TPU v7x, 256 devices: a whole 4x4x8 slice. The times are simulated.
256 devices in a mesh: req: 4 (over x), tp: 64 (over z, y, core).
Axes of the slice: x: 4, y: 4, z: 8, core: 2. Of those that a mesh axis runs over, the one named last changes fastest.
Arguments:
- hidden: bfloat16 [256, 4096], P('req', 'tp'), may hold values from -6 to 6
- norm_gain: bfloat16 [4096], P('tp'), may hold values from 0.099609375 to 1.8984375
- w_qkv: bfloat16 [4096, 5120], P('tp'), may hold values from -0.1875 to 0.1875
- w_out: bfloat16 [4096, 4096], P('tp'), may hold values from -0.09375 to 0.09375
- cache_keys: bfloat16 [4, 65536, 512], P('req', 'tp')
- cache_values: bfloat16 [4, 65536, 512], P('req', 'tp'), may hold values from -6 to 6
- parents: int32 [4, 64], P('req'), may hold values from -1 to 62, as said below
- draft_counts: int32 [4], P('req'), may hold values from 1 to 64, as said below
- cache_lengths: int32 [4], P('req'), may hold values from 1 to 65536, as said below
Outputs:
- updated: bfloat16 [256, 4096], P('req', 'tp')
Inputs may be any that keep to these rules, and one draw needn't show every extreme that they name: parents[r, 0] = -1 and 0 <= parents[r, i] < i for i >= 1. `draft_counts`: some request has all 64 tree tokens live. `cache_lengths`: some request has a full cache of 65536 positions.
All inputs are finite; a program needn't handle non-finite values.
Results may differ from a plain program's by a relative error of at most 0.0065.
The roundings to bfloat16 on the way count: a program that leaves them out, or rounds other values in their place, can miss the bound.
Values may be sent and summed in bfloat16 or wider, within the bound.
No kernel may reach another device: no remote copies, remote signals or barrier semaphores. Data moves between devices by JAX's collectives and lax.ppermute only.
A program may use at most 64 MiB of HBM per device.

v0:
```python
import jax
import jax.numpy as jnp
from jax import lax
from jax.sharding import PartitionSpec as P

HEADS = 32
KV_HEADS = 4
HEAD = 128
NEGATIVE = -1e30


def tree_reach(parents):
    width = parents.shape[1]
    places = jnp.arange(width, dtype=jnp.int32)
    parent_link = (parents[:, :, None] == places[None, None, :]).astype(jnp.float32)
    identity = (places[:, None] == places[None, :]).astype(jnp.float32)
    reached = jnp.minimum(parent_link + identity[None], 1.0)
    for rounds in range(width.bit_length()):
        reached = jnp.minimum(
            jnp.einsum("rij,rjk->rik", reached, reached, precision=lax.Precision.HIGHEST), 1.0
        )
    return reached


def on_device(
    hidden, norm_gain, w_qkv, w_out, cache_keys, cache_values, parents, draft_counts, cache_lengths
):
    tp_count = lax.axis_size("tp")
    tp_rank = lax.axis_index("tp")
    model_width = w_out.shape[1]
    kv_width = KV_HEADS * HEAD
    groups = HEADS // KV_HEADS
    tree = parents.shape[1]
    requests = cache_keys.shape[0]
    places_dev = cache_keys.shape[1]
    inputs = hidden.astype(jnp.float32)
    all_rows = inputs.shape[0]
    own_count = all_rows // tp_count
    scaled = (inputs * norm_gain.astype(jnp.float32)[None, :]).astype(jnp.bfloat16)
    local_squares = jnp.sum(inputs * inputs, axis=1)
    raw, square_sum = lax.psum(
        (jnp.dot(scaled, w_qkv, preferred_element_type=jnp.float32), local_squares), "tp"
    )
    qkv = (raw * lax.rsqrt(square_sum / model_width + 1e-05)[:, None]).astype(jnp.bfloat16)
    query = qkv[:, :model_width]
    own_tokens = lax.dynamic_slice_in_dim(qkv, tp_rank * own_count, own_count, 0)[:, model_width:]
    own_keys = own_tokens[:, :kv_width].reshape(own_count, KV_HEADS, HEAD)
    own_values = own_tokens[:, kv_width:].reshape(own_count, KV_HEADS, HEAD)
    scale = HEAD ** (-0.5)
    key_index = tp_rank * own_count + jnp.arange(own_count, dtype=jnp.int32)
    key_request = key_index // tree
    key_place = key_index % tree
    query_request = jnp.arange(all_rows, dtype=jnp.int32) // tree
    reached = tree_reach(parents).reshape(all_rows, tree)
    column_pick = (jnp.arange(tree, dtype=jnp.int32)[:, None] == key_place[None, :]).astype(
        jnp.float32
    )
    on_path = jnp.dot(reached, column_pick, precision=lax.Precision.HIGHEST) > 0.5
    request_pick = jnp.arange(requests, dtype=jnp.int32)[:, None] == key_request[None, :]
    key_count = jnp.sum(jnp.where(request_pick, draft_counts[:, None], 0), axis=0)
    tree_mask = (
        on_path
        & (query_request[:, None] == key_request[None, :])
        & (key_place < key_count)[None, :]
    )
    query_heads = query.reshape(all_rows, KV_HEADS, groups, HEAD)
    query_blocks = query.reshape(requests, tree, KV_HEADS, groups, HEAD)
    first_place = tp_rank * places_dev
    positions = first_place + jnp.arange(places_dev, dtype=jnp.int32)

    def cache_scores(items):
        queries, keys, length = items
        scores = (
            jnp.einsum(
                "tkgd,pkd->tkgp",
                queries,
                keys.reshape(places_dev, KV_HEADS, HEAD),
                preferred_element_type=jnp.float32,
            )
            * scale
        )
        return jnp.where((positions < length)[None, None, None, :], scores, NEGATIVE)

    stored_scores = lax.map(cache_scores, (query_blocks, cache_keys, cache_lengths))
    tree_scores = (
        jnp.einsum("tkgd,ukd->tkgu", query_heads, own_keys, preferred_element_type=jnp.float32)
        * scale
    )
    tree_scores = jnp.where(tree_mask[:, None, None, :], tree_scores, NEGATIVE)
    local_top = jnp.maximum(
        jnp.max(stored_scores, axis=-1).reshape(all_rows, KV_HEADS, groups),
        jnp.max(tree_scores, axis=-1),
    )
    top = lax.pmax(local_top, "tp")
    top_blocks = top.reshape(requests, tree, KV_HEADS, groups)

    def cache_mix(items):
        block_scores, block_top, values = items
        exponent = jnp.exp(block_scores - block_top[..., None])
        block_totals = jnp.sum(exponent, axis=-1)
        block_mixed = jnp.einsum(
            "tkgp,pkd->tkgd",
            exponent.astype(jnp.bfloat16),
            values.reshape(places_dev, KV_HEADS, HEAD),
            preferred_element_type=jnp.float32,
        )
        return (block_mixed, block_totals)

    mixed, totals = lax.map(cache_mix, (stored_scores, top_blocks, cache_values))
    tree_exp = jnp.exp(tree_scores - top[..., None])
    mixed = mixed.reshape(all_rows, KV_HEADS, groups, HEAD) + jnp.einsum(
        "tkgu,ukd->tkgd",
        tree_exp.astype(jnp.bfloat16),
        own_values,
        preferred_element_type=jnp.float32,
    )
    totals = totals.reshape(all_rows, KV_HEADS, groups) + jnp.sum(tree_exp, axis=-1)
    totals_all = lax.psum(totals.reshape(all_rows, HEADS), "tp")
    mixed_cols = lax.psum_scatter(
        mixed.reshape(all_rows, model_width), "tp", scatter_dimension=1, tiled=True
    )
    columns = w_out.shape[0]
    column_head = (tp_rank * columns + jnp.arange(columns, dtype=jnp.int32)) // HEAD
    head_pick = (jnp.arange(HEADS, dtype=jnp.int32)[:, None] == column_head[None, :]).astype(
        jnp.float32
    )
    column_totals = jnp.dot(totals_all, head_pick, precision=lax.Precision.HIGHEST)
    attended = (mixed_cols / column_totals).astype(jnp.bfloat16)
    partial_terms = jnp.dot(attended, w_out, preferred_element_type=jnp.float32)
    projected = lax.psum_scatter(partial_terms, "tp", scatter_dimension=1, tiled=True)
    return (inputs + projected).astype(jnp.bfloat16)


def solution(mesh):
    placed = (
        P("req", "tp"),
        P("tp"),
        P("tp", None),
        P("tp", None),
        P("req", "tp", None),
        P("req", "tp", None),
        P("req", None),
        P("req"),
        P("req"),
    )
    return jax.shard_map(
        on_device, mesh=mesh, in_specs=placed, out_specs=P("req", "tp"), check_vma=False
    )
```

profile of v0, /device:TPU:2, one launch (start us, length us, event | category | flops | bytes accessed | tf_op | source)
XLA Modules:
  0.0 868.9 jit_solution(1173911116524621926)
XLA Ops:
  6.5 0.0 copy-start
  6.5 0.0 all-reduce.2.cloned.1.call-start
  6.5 0.7 convert_element_type.75
  7.3 0.4 copy-done
  7.6 2.1 fusion.28
  9.7 0.0 all-reduce.2.cloned.1.call-update
  9.8 0.0 reduce-scatter.7.cloned.1.call-start
  9.8 0.8 fusion.24
  11.3 0.8 fusion.27
  12.1 0.2 convolution_minimum_fusion.6
  12.3 0.2 convolution_minimum_fusion.5
  12.5 0.2 convolution_minimum_fusion.4
  12.6 0.2 convolution_minimum_fusion.3
  12.8 0.2 convolution_minimum_fusion.2
  13.0 0.2 convolution_minimum_fusion.1
  13.1 132.0 %psum.22 = f32[64]{0:T(128)S(1)} all-reduce(f32[64]{0:T(128)S(1)} %fusion.24), channel_id=1, replica_groups=mesh['req'=4,'tp'=64] {'tp'}, use_global_device_ids=true, to_apply=%region_2.0 | all-reduce | flops 64 | bytes 512 | tf_op jit(solution)/shard_map/psum | solution.py:41
  145.8 1.3 reshape.297
  147.1 1.3 reshape.299
  148.5 0.2 convolution_minimum_fusion
  148.7 0.1 fusion.15
  148.8 54.3 %all-reduce.2.cloned.1.call-done = f32[64,5120]{1,0:T(8,128)} async-done(((f32[64,5120]{1,0:T(8,128)}), f32[64,5120]{1,0:T(8,128)}) %all-reduce.2.cloned.1.call-update) | async-done | bytes 1310736 | tf_op jit(solution)/shard_map/psum | solution.py:41
  203.1 1.5 multiply_convert_fusion
  204.6 0.1 copy.40
  204.7 2.4 fusion.19
  207.1 4.7 bitcast_reduce_fusion
  211.8 0.1 bitcast_maximum_fusion
  211.9 248.6 %pmax.7 = f32[64,4,8]{2,0,1:T(8,128)S(1)} all-reduce(f32[64,4,8]{2,0,1:T(8,128)S(1)} %bitcast_maximum_fusion), channel_id=1, replica_groups=mesh['req'=4,'tp'=64] {'tp'}, use_global_device_ids=true, to_apply=%region_4.5 | all-reduce | flops 2048 | bytes 16384 | tf_op jit(solution)/shard_map/pmax | solution.py:94
  460.5 0.7 convert_bitcast_fusion
  461.3 0.1 dynamic-slice_convert_fusion
  461.3 4.6 fusion.9
  466.0 0.0 copy-start.2
  466.0 0.0 copy-start.1
  466.0 2.0 copy.38
  468.0 0.0 copy-start.3
  468.0 0.0 reduce-scatter.7.cloned.1.call-update
  468.1 0.0 reduce-scatter.9.cloned.1.call-start
  468.1 4.5 fusion.1
  472.6 0.1 copy.24
  472.7 0.0 copy-done.2
  472.7 0.1 copy.25
  472.8 246.3 %psum.23 = f32[64,32]{0,1:T(8,128)S(1)} all-reduce(f32[64,32]{0,1:T(8,128)S(1)} %bitcast_add_fusion), channel_id=1, replica_groups=mesh['req'=4,'tp'=64] {'tp'}, use_global_device_ids=true, to_apply=%region_7.8 | all-reduce | flops 2048 | bytes 16384 | tf_op jit(solution)/shard_map/psum | solution.py:118
  719.1 0.0 reduce-scatter.7.cloned.1.call-done
  719.1 0.8 copy.35
  719.9 0.2 fusion.12
  720.1 0.0 copy-done.1
  720.2 1.9 convolution_bitcast_fusion
  722.0 0.0 reduce-scatter.9.cloned.1.call-update
  722.1 138.9 %reduce-scatter.9.cloned.1.call-done = f32[64,64]{1,0:T(8,128)} async-done(((f32[4096,64]{1,0:T(8,128)}), f32[64,64]{1,0:T(8,128)}) %reduce-scatter.9.cloned.1.call-update) | async-done | bytes 16400
  860.9 0.8 copy.37
  861.8 0.0 copy-done.3
  861.8 0.6 fusion.25
  (5 shorter events, 0.1 us)
Async XLA Ops:
  6.5 1.1 copy-start
  6.5 196.5 %all-reduce.2.cloned.1.call-start = ((), (), s32[]{:S(2)}) async-start(), calls=%async_computation.2 | async-start | bytes 2621440 | tf_op jit(solution)/shard_map/psum | solution.py:41
  9.8 709.3 %reduce-scatter.7.cloned.1.call-start = ((), (), s32[]{:S(2)}) async-start(), calls=%async_computation.3 | async-start | bytes 2129920
  466.0 6.7 copy-start.2
  466.0 254.1 %copy-start.1 = (bf16[64,4096]{1,0:T(8,128)(2,1)S(1)}, bf16[64,4096]{1,0:T(8,128)(2,1)}, u32[]{:S(2)}) copy-start(bf16[64,4096]{1,0:T(8,128)(2,1)} %param.12) | copy-start | bytes 1572868
  468.0 393.7 %copy-start.3 = (bf16[64,64]{1,0:T(8,128)(2,1)S(1)}, bf16[64,64]{1,0:T(8,128)(2,1)}, u32[]{:S(2)}) copy-start(bf16[64,64]{1,0:T(8,128)(2,1)} %param.9) | copy-start | bytes 24580
  468.1 392.9 %reduce-scatter.9.cloned.1.call-start = ((), (), s32[]{:S(2)}) async-start(), calls=%async_computation.4 | async-start | bytes 2129920
Sparse Core Ops, SparseCore 0:
  10.8 192.2 all-reduce.1
  468.2 138.6 reduce-scatter.6
  722.2 138.7 reduce-scatter.8
where the time goes:
time: 869 us
  blocking collectives  627 us (72%)
  waiting for transfers between devices  193 us (22%)
  matrix products  17.3 us (2%)
  between operations  14.6 us (2%)
  other arithmetic  9.83 us (1%)
    pmax x1, blocking collectives, on_device(): top = lax.pmax(local_top, 'tp')  249 us
    psum x1, blocking collectives, on_device(): totals_all = lax.psum(totals.reshape(all_rows, HEADS), 'tp')  246 us
    unnamed x5, waiting for transfers between devices  139 us
    psum x1, blocking collectives, on_device(): lax.psum((jnp.dot(scaled, w_qkv, preferred_element_type=jnp.float32), loc...  132 us
    psum x1, waiting for transfers between devices, on_device(): lax.psum((jnp.dot(scaled, w_qkv, preferred_element_type=jnp.float32), loc...  54.3 us
  transfers between devices with their start and end apart: 3, of which 2 were waited for; matrix products, arithmetic and copies ran while one was open for 1% of the time, Pallas kernels for 0%

commit v1 on v0

--- a/solution.py
+++ b/solution.py
@@ -1,3 +1,4 @@
+import functools
 import jax
 import jax.numpy as jnp
 from jax import lax
@@ -7,6 +8,14 @@
 KV_HEADS = 4
 HEAD = 128
 NEGATIVE = -1e30
+
+
+def pass_case_all(local, named_axis):
+    prior = jnp.sum(lax.all_gather(local, named_axis), axis=0)
+    return prior
+
+
+choose_page = functools.partial(pass_case_all, named_axis="tp")
 
 
 def tree_reach(parents):
@@ -115,7 +124,7 @@
         preferred_element_type=jnp.float32,
     )
     totals = totals.reshape(all_rows, KV_HEADS, groups) + jnp.sum(tree_exp, axis=-1)
-    totals_all = lax.psum(totals.reshape(all_rows, HEADS), "tp")
+    totals_all = choose_page(totals.reshape(all_rows, HEADS))
     mixed_cols = lax.psum_scatter(
         mixed.reshape(all_rows, model_width), "tp", scatter_dimension=1, tiled=True
     )

time: 869 us -> 759 us (0.87)
  blocking collectives: 627 us -> 428 us
  waiting for transfers between devices: 193 us -> 282 us
    psum x1 -> x0, blocking collectives: 246 us -> none  [on_device(): totals_all = lax.psum(totals.reshape(all_rows, HEADS), 'tp')]
    unnamed x5, waiting for transfers between devices: 139 us -> 228 us
    all_gather x0 -> x1, blocking collectives: none -> 47.2 us  [pass_case_all(): prior = jnp.sum(lax.all_gather(local, named_axis), axis=0)]
  transfers between devices with their start and end apart: 3 -> 3, of which waited for: 2 -> 3; matrix products, arithmetic and copies ran while one was open for 1% -> 1% of each run, Pallas kernels for 0% -> 0%
where the time goes in v1:
time: 759 us
  blocking collectives  428 us (56%)
  waiting for transfers between devices  282 us (37%)
  matrix products  17.3 us (2%)
  between operations  14.6 us (2%)
  other arithmetic  9.93 us (1%)
    pmax x1, blocking collectives, on_device(): top = lax.pmax(local_top, 'tp')  249 us
    unnamed x5, waiting for transfers between devices  228 us
    psum x1, blocking collectives, on_device(): lax.psum((jnp.dot(scaled, w_qkv, preferred_element_type=jnp.float32), loc...  132 us
    psum x1, waiting for transfers between devices, on_device(): lax.psum((jnp.dot(scaled, w_qkv, preferred_element_type=jnp.float32), loc...  54.3 us
    all_gather x1, blocking collectives, pass_case_all(): prior = jnp.sum(lax.all_gather(local, named_axis), axis=0)  47.2 us
  transfers between devices with their start and end apart: 3, of which 3 were waited for; matrix products, arithmetic and copies ran while one was open for 1% of the time, Pallas kernels for 0%

profile of v1, /device:TPU:2, one launch (start us, length us, event | category | flops | bytes accessed | tf_op | source)
XLA Modules:
  0.0 758.7 jit_solution(14692439131608582330)
XLA Ops:
  6.5 0.0 copy-start
  6.5 0.0 all-reduce.2.cloned.1.call-start
  6.5 0.7 convert_element_type.75
  7.3 0.4 copy-done
  7.6 2.1 fusion.28
  9.7 0.0 all-reduce.2.cloned.1.call-update
  9.8 0.0 reduce-scatter.7.cloned.1.call-start
  9.8 0.8 fusion.24
  11.3 0.8 fusion.27
  12.1 0.2 convolution_minimum_fusion.6
  12.3 0.2 convolution_minimum_fusion.5
  12.5 0.2 convolution_minimum_fusion.4
  12.6 0.2 convolution_minimum_fusion.3
  12.8 0.2 convolution_minimum_fusion.2
  13.0 0.2 convolution_minimum_fusion.1
  13.1 132.0 %psum.15 = f32[64]{0:T(128)S(1)} all-reduce(f32[64]{0:T(128)S(1)} %fusion.24), channel_id=1, replica_groups=mesh['req'=4,'tp'=64] {'tp'}, use_global_device_ids=true, to_apply=%region_2.0 | all-reduce | flops 64 | bytes 512 | tf_op jit(solution)/shard_map/psum | solution.py:50
  145.8 1.3 reshape.311
  147.1 1.3 reshape.313
  148.5 0.2 convolution_minimum_fusion
  148.7 0.1 fusion.15
  148.8 54.3 %all-reduce.2.cloned.1.call-done = f32[64,5120]{1,0:T(8,128)} async-done(((f32[64,5120]{1,0:T(8,128)}), f32[64,5120]{1,0:T(8,128)}) %all-reduce.2.cloned.1.call-update) | async-done | bytes 1310736 | tf_op jit(solution)/shard_map/psum | solution.py:50
  203.1 1.5 multiply_convert_fusion
  204.6 0.1 copy.40
  204.7 2.4 fusion.19
  207.1 4.7 bitcast_reduce_fusion
  211.8 0.1 bitcast_maximum_fusion
  211.9 248.6 %pmax.7 = f32[64,4,8]{2,0,1:T(8,128)S(1)} all-reduce(f32[64,4,8]{2,0,1:T(8,128)S(1)} %bitcast_maximum_fusion), channel_id=1, replica_groups=mesh['req'=4,'tp'=64] {'tp'}, use_global_device_ids=true, to_apply=%region_4.5 | all-reduce | flops 2048 | bytes 16384 | tf_op jit(solution)/shard_map/pmax | solution.py:103
  460.5 0.7 convert_bitcast_fusion
  461.3 0.1 dynamic-slice_convert_fusion
  461.3 4.6 fusion.9
  466.0 0.0 copy-start.2
  466.0 0.0 copy-start.1
  466.0 2.0 copy.38
  468.0 0.0 reduce-scatter.7.cloned.1.call-update
  468.1 0.0 copy-start.3
  468.1 0.0 reduce-scatter.9.cloned.1.call-start
  468.2 4.5 fusion.1
  472.6 0.1 copy.24
  472.7 0.0 copy-done.2
  472.7 0.1 copy.25
  472.8 47.2 %all_gather.3 = f32[64,64,32]{1,2,0:T(8,128)S(1)} all-gather(f32[1,64,32]{1,2,0:T(8,128)S(1)} %bitcast_add_fusion), channel_id=1, replica_groups=mesh['req'=4,'tp'=64] {'tp'}, dimensions={0}, use_global_device_ids=true | all-gather | bytes 532480 | tf_op jit(solution)/shard_map/all_gather | solution.py:14
  520.0 0.1 reduce_sum.41
  520.1 86.8 %reduce-scatter.7.cloned.1.call-done = f32[64,64]{1,0:T(8,128)} async-done(((f32[4096,64]{1,0:T(8,128)}), f32[64,64]{1,0:T(8,128)}) %reduce-scatter.7.cloned.1.call-update) | async-done | bytes 16400
  606.9 0.8 copy.35
  607.7 0.2 fusion.12
  607.9 0.0 copy-done.1
  607.9 1.9 convolution_bitcast_fusion
  609.8 0.0 reduce-scatter.9.cloned.1.call-update
  609.9 140.9 %reduce-scatter.9.cloned.1.call-done = f32[64,64]{1,0:T(8,128)} async-done(((f32[4096,64]{1,0:T(8,128)}), f32[64,64]{1,0:T(8,128)}) %reduce-scatter.9.cloned.1.call-update) | async-done | bytes 16400
  750.7 0.8 copy.37
  751.6 0.0 copy-done.3
  751.6 0.6 fusion.25
  (5 shorter events, 0.1 us)
Async XLA Ops:
  6.5 1.1 copy-start
  6.5 196.5 %all-reduce.2.cloned.1.call-start = ((), (), s32[]{:S(2)}) async-start(), calls=%async_computation.2 | async-start | bytes 2621440 | tf_op jit(solution)/shard_map/psum | solution.py:50
  9.8 597.1 %reduce-scatter.7.cloned.1.call-start = ((), (), s32[]{:S(2)}) async-start(), calls=%async_computation.3 | async-start | bytes 2129920
  466.0 6.7 copy-start.2
  466.0 141.9 %copy-start.1 = (bf16[64,4096]{1,0:T(8,128)(2,1)S(1)}, bf16[64,4096]{1,0:T(8,128)(2,1)}, u32[]{:S(2)}) copy-start(bf16[64,4096]{1,0:T(8,128)(2,1)} %param.12) | copy-start | bytes 1572868
  468.1 283.5 %copy-start.3 = (bf16[64,64]{1,0:T(8,128)(2,1)S(1)}, bf16[64,64]{1,0:T(8,128)(2,1)}, u32[]{:S(2)}) copy-start(bf16[64,64]{1,0:T(8,128)(2,1)} %param.9) | copy-start | bytes 24580
  468.1 282.7 %reduce-scatter.9.cloned.1.call-start = ((), (), s32[]{:S(2)}) async-start(), calls=%async_computation.4 | async-start | bytes 2129920
Sparse Core Ops, SparseCore 0:
  10.8 192.2 all-reduce.1
  468.2 138.6 reduce-scatter.6
  610.9 139.7 reduce-scatter.8
